TPU v7x, 512 devices: a whole 4x8x8 slice. The times are simulated.
512 devices in a mesh: band: 32 (over x, y), seq: 16 (over z, core).
Axes of the slice: x: 4, y: 8, z: 8, core: 2. Of those that a mesh axis runs over, the one named last changes fastest.
Arguments:
- posteriors: bfloat16 [32, 262144], P(None, ('band', 'seq'))
- seed_mask: int32 [262144], P(('band', 'seq')), may hold values 0 or 1
- frame_perm: int32 [512, 512], P(('band', 'seq')), may hold values from 0 to 511, each once within a row
- lengths: int32 [256], replicated, may hold values from 1 to 4096, 262144 in all
- embeddings: bfloat16 [262144, 256], P(('band', 'seq')), may hold values from -12 to 12
- partners: int32 [2048, 32], P(('band', 'seq')), may hold values from 0 to 127, as said below
- levels: int32 [2048, 32], P(('band', 'seq')), may hold values from 1 to 8, as said below
Outputs:
- spread_labels: float32 [32, 262144], P(None, ('band', 'seq'))
Inputs may be any that keep to these rules, and one draw needn't show every extreme that they name: `partners`: within each seq index s, slot k pairs the 128 tiles mutually: if tile number a names b in slot k then b names a in slot k; no tile names itself. `levels`: two tiles paired in slot k carry the same level.
All inputs are finite; a program needn't handle non-finite values. No bound on the sum of `seed_mask` on one device may be relied on, other than what follows from the above.
Results may differ from a plain program's by a relative error of at most 0.007.
Values may be sent and summed in bfloat16 or wider, within the bound.
No kernel may reach another device: no remote copies, remote signals or barrier semaphores. Data moves between devices by JAX's collectives and lax.ppermute only.
A program may use at most 64 MiB of HBM per device.

v0:
```python
import math
import jax
import jax.numpy as jnp
from jax import lax
from jax.sharding import PartitionSpec as P

RADIUS = 64
ITERS = 3
decay_len = 16.0
spread_rate = 0.9


def with_halo(cells, sides, width):
    for axis, dim in sides:
        count = lax.axis_size(axis)
        ends = count - 1
        head = lax.slice_in_dim(cells, 0, width, axis=dim)
        tail = lax.slice_in_dim(cells, cells.shape[dim] - width, cells.shape[dim], axis=dim)
        cells = jnp.concatenate(
            [
                lax.ppermute(tail, axis, [(i, (i + 1) % count) for i in range(ends)]),
                cells,
                lax.ppermute(head, axis, [((i + 1) % count, i) for i in range(ends)]),
            ],
            axis=dim,
        )
    return cells


def total_over_devices(values):
    for axis in ("seq", "band"):
        count = lax.axis_size(axis)
        spread = jnp.broadcast_to(values[None], (count,) + values.shape)
        rows = lax.all_to_all(spread, axis, split_axis=0, concat_axis=0, tiled=True)
        values = jnp.sum(rows, axis=0)
    return values


def band_gather(block):
    count = lax.axis_size("band")
    spread = jnp.broadcast_to(block[None], (count,) + block.shape)
    return lax.all_to_all(spread, "band", split_axis=0, concat_axis=0, tiled=True)


def on_device(posteriors, seed_mask, frame_perm, lengths, embeddings, partners, levels):
    channels, frames = posteriors.shape
    band_count = lax.axis_size("band")
    groups = lax.axis_size("seq")
    tile_count = frames // 128
    seeded = posteriors * seed_mask.astype(jnp.bfloat16)[None, :]
    ordered = jnp.take(seeded, frame_perm[0], axis=1).reshape(
        channels, band_count, frames // band_count
    )
    arrived = lax.all_to_all(ordered, "band", split_axis=1, concat_axis=1, tiled=True)
    labels = arrived.reshape(channels, frames).astype(jnp.float32)
    device = lax.axis_index("band") * groups + lax.axis_index("seq")
    frame_total = frames * band_count * groups
    window = 128 + 2 * RADIUS
    global_at = device * frames - RADIUS + jnp.arange(frames + 2 * RADIUS, dtype=jnp.int32)
    utt_ends = jnp.cumsum(lengths)
    owner_seg = jnp.sum((utt_ends[None, :] <= global_at[:, None]).astype(jnp.int32), axis=1)
    inside = (global_at >= 0) & (global_at < frame_total)
    tile_off = (jnp.arange(tile_count, dtype=jnp.int32) * 128)[:, None, None]
    win_pos = tile_off + jnp.arange(window, dtype=jnp.int32)[None, :, None]
    row_pos = tile_off + RADIUS + jnp.arange(128, dtype=jnp.int32)[None, None, :]
    offset = jnp.abs(win_pos - row_pos)
    linked = (
        (offset >= 1)
        & (offset <= RADIUS)
        & (owner_seg[win_pos] == owner_seg[row_pos])
        & inside[win_pos]
    )
    band_tiles = jnp.where(
        linked, jnp.exp(-offset.astype(jnp.float32) / decay_len), jnp.float32(0.0)
    ).astype(jnp.bfloat16)
    near_degree = jnp.sum(band_tiles.astype(jnp.float32), axis=1).reshape(frames)
    gathered = lax.all_gather(embeddings, "band", axis=0, tiled=True)
    labels_band = band_gather(arrived.reshape(channels, frames))
    labels_band, gathered = lax.optimization_barrier((labels_band, gathered))
    embed_width = embeddings.shape[1]
    partner_rows = gathered.reshape(-1, 128, embed_width)[partners]
    own_rows = embeddings.reshape(tile_count, 128, embed_width)
    inner_prod = jnp.einsum(
        "tkje,tie->tkji", partner_rows, own_rows, preferred_element_type=jnp.float32
    )
    affinity = (
        jnp.exp(0.5 * (inner_prod / math.sqrt(embed_width)))
        * (levels.astype(jnp.float32) / 8.0)[:, :, None, None]
        / 128.0
    )
    affinity = affinity.astype(jnp.bfloat16)
    far_degree = jnp.sum(affinity.astype(jnp.float32), axis=(1, 2)).reshape(frames)
    norm_scale = 1.0 / jnp.sqrt(near_degree + far_degree)

    def squares(residual):
        return total_over_devices(jnp.sum(residual * residual, axis=1))

    solution = jnp.zeros((channels, frames), jnp.float32)
    residual = labels
    direction = labels
    first_norm = jnp.sum(residual * residual, axis=1)
    scale_band = band_gather(norm_scale)
    for iteration in range(ITERS):
        lifted = (norm_scale[None, :] * direction).astype(jnp.bfloat16)
        padded = with_halo(lifted, ((("band", "seq"), 1),), RADIUS)
        windows = jnp.stack(
            [padded[:, position * 128 : position * 128 + window] for position in range(tile_count)],
            axis=0,
        )
        near_term = jnp.einsum(
            "tcw,twa->cta", windows, band_tiles, preferred_element_type=jnp.float32
        ).reshape(channels, frames)
        if iteration == 0:
            lifted_band = (scale_band[:, None, :] * labels_band.astype(jnp.float32)).astype(
                jnp.bfloat16
            )
        else:
            lifted_band = band_gather(lifted)
        spread = jnp.transpose(lifted_band, (1, 0, 2)).reshape(channels, -1, 128)
        far_tiles = spread[:, partners]
        far_term = jnp.einsum(
            "ctkj,tkji->cti", far_tiles, affinity, preferred_element_type=jnp.float32
        ).reshape(channels, frames)
        image = direction - spread_rate * norm_scale[None, :] * (near_term + far_term)
        sums = [jnp.sum(direction * image, axis=1)]
        last = iteration == ITERS - 1
        if not last:
            sums += [jnp.sum(residual * image, axis=1), jnp.sum(image * image, axis=1)]
        if iteration == 0:
            sums.append(first_norm)
        totals = total_over_devices(jnp.stack(sums))
        curve = totals[0]
        if iteration == 0:
            norm_now = totals[-1]
        alpha = norm_now / curve
        solution = solution + alpha[:, None] * direction
        if not last:
            residual = residual - alpha[:, None] * image
            norm_next = norm_now - 2.0 * alpha * totals[1] + alpha * alpha * totals[2]
            direction = residual + (norm_next / norm_now)[:, None] * direction
            norm_now = norm_next
    return solution


def solution(mesh):
    placed = (
        P(None, ("band", "seq")),
        P(("band", "seq")),
        P(("band", "seq"), None),
        P(),
        P(("band", "seq"), None),
        P(("band", "seq"), None),
        P(("band", "seq"), None),
    )
    return jax.shard_map(
        on_device, mesh=mesh, in_specs=placed, out_specs=P(None, ("band", "seq")), check_vma=False
    )
```

profile of v0, /device:TPU:1, one launch (start us, length us, event | category | flops | bytes accessed | tf_op | source)
XLA Modules:
  0.0 341.7 jit_solution(14593774616092935248)
XLA Ops:
  6.5 0.7 all-gather.2.cloned.1.call-update
  7.3 0.7 convert_element_type.66
  7.9 0.8 broadcast_multiply_fusion
  9.4 1.3 reduce.14
  10.8 0.7 compare_select_fusion.1
  11.5 1.3 gather_fusion
  13.0 0.8 reshape.829
  13.7 10.5 %all-to-all-start = ((bf16[32,2,256]{2,1,0:T(2,128)(2,1)}), bf16[32,2,256]{2,1,0:T(2,128)(2,1)S(1)}, u32[]{:S(2)}, u32[]{:S(2)}) async-start(bf16[32,2,256]{2,1,0:T(2,128)(2,1)} %reshape.829), calls=%async_computation | async-start | bytes 65536 | tf_op jit(solution)/shard_map/all_to_all | solution.py:54
  24.3 1.0 reduce-window.9
  25.6 7.4 %all-to-all-done = bf16[32,2,256]{2,1,0:T(2,128)(2,1)S(1)} async-done(((bf16[32,2,256]{2,1,0:T(2,128)(2,1)}), bf16[32,2,256]{2,1,0:T(2,128)(2,1)S(1)}, u32[]{:S(2)}, u32[]{:S(2)}) %all-to-all-start) | async-done | bytes 32800 | tf_op jit(solution)/shard_map/all_to_all | solution.py:54
  33.2 1.2 broadcast_in_dim.40
  34.4 3.9 %all-to-all-start.1 = ((bf16[32,32,512]{2,1,0:T(8,128)(2,1)}), bf16[32,32,512]{2,1,0:T(8,128)(2,1)S(1)}, u32[]{:S(2)}, u32[]{:S(2)}) async-start(bf16[32,32,512]{2,1,0:T(8,128)(2,1)} %broadcast_in_dim.40), calls=%async_computation.1 | async-start | bytes 2097152 | tf_op jit(solution)/shard_map/all_to_all | solution.py:42
  38.7 4.5 %gather_fusion.1 = s32[1024]{0:T(1024)S(1)} fusion(s32[640]{0:T(1024)S(1)} %convert_reduce_fusion.1, s32[1024]{0:T(1024)S(1)} %broadcast_clamp_fusion), kind=kCustom, calls=%fused_computation.1 | custom fusion | bytes 12288 | tf_op jit(solution)/shard_map/gather | solution.py:70
  43.3 2.3 gather_fusion.2
  45.6 6.8 %gather_fusion.3 = pred[1024]{0:T(1024)(128)(4,1)S(1)} fusion(pred[640]{0:T(1024)(128)(4,1)S(1)} %compare_and_fusion.1, s32[1024]{0:T(1024)S(1)} %broadcast_clamp_fusion), kind=kCustom, calls=%fused_computation.3 | custom fusion | bytes 6144 | tf_op jit(solution)/shard_map/gather | solution.py:71
  53.3 16.7 %all-to-all-done.1 = bf16[32,32,512]{2,1,0:T(8,128)(2,1)S(1)} async-done(((bf16[32,32,512]{2,1,0:T(8,128)(2,1)}), bf16[32,32,512]{2,1,0:T(8,128)(2,1)S(1)}, u32[]{:S(2)}, u32[]{:S(2)}) %all-to-all-start.1) | async-done | bytes 1048608 | tf_op jit(solution)/shard_map/all_to_all | solution.py:42
  70.0 58.1 %all-gather.2.cloned.1.call-done = bf16[16384,256]{1,0:T(8,128)(2,1)} async-done(((bf16[512,256]{1,0:T(8,128)(2,1)}), bf16[16384,256]{1,0:T(8,128)(2,1)}) %all-gather.2.cloned.1.call-update) | async-done | bytes 8388624 | tf_op jit(solution)/shard_map/all_gather | solution.py:77
  128.2 10.0 %gather_fusion.4 = bf16[128,128,256]{2,1,0:T(8,128)(2,1)} fusion(bf16[128,128,256]{2,1,0:T(8,128)(2,1)} %bitcast.181, s32[1024]{0:T(1024)S(1)} %pad_clamp_fusion), kind=kCustom, calls=%fused_computation.4 | custom fusion | bytes 16777728 | tf_op jit(solution)/shard_map/gather | solution.py:81
  138.1 7.7 %convert_reduce_fusion = (f32[4,128]{1,0:T(4,128)S(1)}, bf16[4,32,128,128]{3,2,1,0:T(8,128)(2,1)}) fusion(f32[4,32]{1,0:T(4,128)S(1)} %convert_multiply_fusion.6, bf16[4,32,128,256]{3,2,1,0:T(8,128)(2,1)} %bitcast.182, bf16[4,128,256,1]{2,1,3,0:T(8,128)(2,1)S(1)} %bitcast.198), kind=kOutput, calls=%fused_computation.8 | convolution fusion | flops 1086324224 | bytes 12847616 | tf_op jit(solution)/shard_map/tkje,tie->tkji/dot_general | solution.py:83
  145.9 4.2 %collective-permute-start = (bf16[32,64]{1,0:T(8,128)(2,1)S(1)}, bf16[32,64]{1,0:T(8,128)(2,1)S(1)}, u32[]{:S(2)}, u32[]{:S(2)}) collective-permute-start(bf16[32,64]{1,0:T(8,128)(2,1)S(1)} %get-tuple-element.41), channel_id=1, source_target_pairs={{0,1},{1,2},{2,3},{3,4},{4,5},{5,6},{6,7},{7,8},{8,9},{9,10},{10,1... | collective-permute-start | bytes 12296 | tf_op jit(solution)/shard_map/ppermute | solution.py:21
  150.2 1.9 collective-permute-start.1
  152.8 5.7 %all-to-all-start.2 = ((f32[32,1,512]{2,1,0:T(1,128)}), f32[32,1,512]{2,1,0:T(1,128)S(1)}, u32[]{:S(2)}, u32[]{:S(2)}) async-start(f32[32,1,512]{2,1,0:T(1,128)} %mul.397), calls=%async_computation.2 | async-start | bytes 131072 | tf_op jit(solution)/shard_map/all_to_all | solution.py:42
  159.2 7.9 %all-to-all-done.2 = f32[32,1,512]{2,1,0:T(1,128)S(1)} async-done(((f32[32,1,512]{2,1,0:T(1,128)}), f32[32,1,512]{2,1,0:T(1,128)S(1)}, u32[]{:S(2)}, u32[]{:S(2)}) %all-to-all-start.2) | async-done | bytes 65568 | tf_op jit(solution)/shard_map/all_to_all | solution.py:42
  169.3 0.8 gather_fusion.5
  170.1 2.9 fusion.3
  173.5 17.3 %all_to_all.56 = f32[16,1,128]{2,1,0:T(1,128)S(1)} all-to-all(f32[16,1,128]{2,1,0:T(1,128)S(1)} %reshape.831), channel_id=1, replica_groups=mesh['band'=32,'seq'=16] {'seq'}, dimensions={0} | all-to-all | bytes 16384 | tf_op jit(solution)/shard_map/all_to_all | solution.py:34
  192.2 11.6 %all_to_all.57 = f32[32,1,128]{2,1,0:T(1,128)S(1)} all-to-all(f32[32,1,128]{2,1,0:T(1,128)S(1)} %reshape.833), channel_id=1, replica_groups=mesh['band'=32,'seq'=16] {'band'}, dimensions={0} | all-to-all | bytes 32768 | tf_op jit(solution)/shard_map/all_to_all | solution.py:34
  204.8 1.1 broadcast_in_dim.44
  205.9 3.9 %all-to-all-start.5 = ((bf16[32,32,512]{2,1,0:T(8,128)(2,1)}), bf16[32,32,512]{2,1,0:T(8,128)(2,1)S(1)}, u32[]{:S(2)}, u32[]{:S(2)}) async-start(bf16[32,32,512]{2,1,0:T(8,128)(2,1)} %broadcast_in_dim.44), calls=%async_computation.5 | async-start | bytes 2097152 | tf_op jit(solution)/shard_map/all_to_all | solution.py:42
  209.9 4.0 %collective-permute-start.2 = (bf16[32,64]{1,0:T(8,128)(2,1)S(1)}, bf16[32,64]{1,0:T(8,128)(2,1)S(1)}, u32[]{:S(2)}, u32[]{:S(2)}) collective-permute-start(bf16[32,64]{1,0:T(8,128)(2,1)S(1)} %get-tuple-element.35), channel_id=1, source_target_pairs={{0,1},{1,2},{2,3},{3,4},{4,5},{5,6},{6,7},{7,8},{8,9},{9,10},{10,1... | collective-permute-start | bytes 12296 | tf_op jit(solution)/shard_map/ppermute | solution.py:21
  213.9 1.9 collective-permute-start.3
  215.8 3.3 collective-permute-done.3
  219.9 14.5 %all-to-all-done.5 = bf16[32,32,512]{2,1,0:T(8,128)(2,1)S(1)} async-done(((bf16[32,32,512]{2,1,0:T(8,128)(2,1)}), bf16[32,32,512]{2,1,0:T(8,128)(2,1)S(1)}, u32[]{:S(2)}, u32[]{:S(2)}) %all-to-all-start.5) | async-done | bytes 1048608 | tf_op jit(solution)/shard_map/all_to_all | solution.py:42
  236.3 0.8 gather_fusion.6
  237.0 2.9 fusion.2
  240.4 15.1 %all_to_all.58 = f32[16,3,32]{2,1,0:T(4,128)S(1)} all-to-all(f32[16,3,32]{2,1,0:T(4,128)S(1)} %broadcast_in_dim.45), channel_id=1, replica_groups=mesh['band'=32,'seq'=16] {'seq'}, dimensions={0} | all-to-all | bytes 12288 | tf_op jit(solution)/shard_map/all_to_all | solution.py:34
  255.5 14.1 %all_to_all.59 = f32[32,3,32]{2,1,0:T(4,128)S(1)} all-to-all(f32[32,3,32]{2,1,0:T(4,128)S(1)} %broadcast_in_dim.46), channel_id=1, replica_groups=mesh['band'=32,'seq'=16] {'band'}, dimensions={0} | all-to-all | bytes 24576 | tf_op jit(solution)/shard_map/all_to_all | solution.py:34
  269.8 1.1 broadcast_in_dim.47
  270.9 3.9 %all-to-all-start.8 = ((bf16[32,32,512]{2,1,0:T(8,128)(2,1)}), bf16[32,32,512]{2,1,0:T(8,128)(2,1)S(1)}, u32[]{:S(2)}, u32[]{:S(2)}) async-start(bf16[32,32,512]{2,1,0:T(8,128)(2,1)} %broadcast_in_dim.47), calls=%async_computation.8 | async-start | bytes 2097152 | tf_op jit(solution)/shard_map/all_to_all | solution.py:42
  274.9 3.9 %collective-permute-start.4 = (bf16[32,64]{1,0:T(8,128)(2,1)S(1)}, bf16[32,64]{1,0:T(8,128)(2,1)S(1)}, u32[]{:S(2)}, u32[]{:S(2)}) collective-permute-start(bf16[32,64]{1,0:T(8,128)(2,1)S(1)} %get-tuple-element.29), channel_id=1, source_target_pairs={{0,1},{1,2},{2,3},{3,4},{4,5},{5,6},{6,7},{7,8},{8,9},{9,10},{10,1... | collective-permute-start | bytes 12296 | tf_op jit(solution)/shard_map/ppermute | solution.py:21
  278.8 2.1 collective-permute-start.5
  280.9 3.1 collective-permute-done.5
  284.7 14.7 %all-to-all-done.8 = bf16[32,32,512]{2,1,0:T(8,128)(2,1)S(1)} async-done(((bf16[32,32,512]{2,1,0:T(8,128)(2,1)}), bf16[32,32,512]{2,1,0:T(8,128)(2,1)S(1)}, u32[]{:S(2)}, u32[]{:S(2)}) %all-to-all-start.8) | async-done | bytes 1048608 | tf_op jit(solution)/shard_map/all_to_all | solution.py:42
  301.4 0.8 gather_fusion.7
  302.1 2.9 fusion.1
  305.5 14.7 %all_to_all.60 = f32[16,1,32]{2,1,0:T(1,128)S(1)} all-to-all(f32[16,1,32]{2,1,0:T(1,128)S(1)} %broadcast_in_dim.48), channel_id=1, replica_groups=mesh['band'=32,'seq'=16] {'seq'}, dimensions={0} | all-to-all | bytes 4096 | tf_op jit(solution)/shard_map/all_to_all | solution.py:34
  320.2 13.9 %all_to_all.61 = f32[32,1,32]{2,1,0:T(1,128)S(1)} all-to-all(f32[32,1,32]{2,1,0:T(1,128)S(1)} %broadcast_in_dim.49), channel_id=1, replica_groups=mesh['band'=32,'seq'=16] {'band'}, dimensions={0} | all-to-all | bytes 8192 | tf_op jit(solution)/shard_map/all_to_all | solution.py:34
  334.1 0.7 fusion.19
  (99 shorter events, 15.5 us)
Async XLA Ops:
  6.5 45.9 %copy-start.1 = (s32[4,32]{1,0:T(4,128)S(1)}, s32[4,32]{1,0:T(4,128)}, u32[]{:S(2)}) copy-start(s32[4,32]{1,0:T(4,128)} %param.12) | copy-start | bytes 1540
  6.5 46.7 %copy-start.2 = (s32[4,32]{1,0:T(4,128)S(1)}, s32[4,32]{1,0:T(4,128)}, u32[]{:S(2)}) copy-start(s32[4,32]{1,0:T(4,128)} %param.13) | copy-start | bytes 1540
  6.5 121.6 %all-gather.2.cloned.1.call-start = ((), (), s32[]{:S(2)}) async-start(), calls=%async_computation.11 | async-start | bytes 8650752 | tf_op jit(solution)/shard_map/all_gather | solution.py:77
  13.7 19.3 %all-to-all-start = ((bf16[32,2,256]{2,1,0:T(2,128)(2,1)}), bf16[32,2,256]{2,1,0:T(2,128)(2,1)S(1)}, u32[]{:S(2)}, u32[]{:S(2)}) async-start(bf16[32,2,256]{2,1,0:T(2,128)(2,1)} %reshape.829), calls=%async_computation | async-start | bytes 65536 | tf_op jit(solution)/shard_map/all_to_all | solution.py:54
  34.4 35.6 %all-to-all-start.1 = ((bf16[32,32,512]{2,1,0:T(8,128)(2,1)}), bf16[32,32,512]{2,1,0:T(8,128)(2,1)S(1)}, u32[]{:S(2)}, u32[]{:S(2)}) async-start(bf16[32,32,512]{2,1,0:T(8,128)(2,1)} %broadcast_in_dim.40), calls=%async_computation.1 | async-start | bytes 2097152 | tf_op jit(solution)/shard_map/all_to_all | solution.py:42
  128.1 10.0 %copy-start = (bf16[512,256]{1,0:T(8,128)(2,1)S(1)}, bf16[512,256]{1,0:T(8,128)(2,1)}, u32[]{:S(2)}) copy-start(bf16[512,256]{1,0:T(8,128)(2,1)} %param.11) | copy-start | bytes 786436
  145.9 12.6 %collective-permute-start = (bf16[32,64]{1,0:T(8,128)(2,1)S(1)}, bf16[32,64]{1,0:T(8,128)(2,1)S(1)}, u32[]{:S(2)}, u32[]{:S(2)}) collective-permute-start(bf16[32,64]{1,0:T(8,128)(2,1)S(1)} %get-tuple-element.41), channel_id=1, source_target_pairs={{0,1},{1,2},{2,3},{3,4},{4,5},{5,6},{6,7},{7,8},{8,9},{9,10},{10,1... | collective-permute-start | bytes 12296 | tf_op jit(solution)/shard_map/ppermute | solution.py:21
  150.2 8.4 %collective-permute-start.1 = (bf16[32,64]{1,0:T(8,128)(2,1)S(1)}, bf16[32,64]{1,0:T(8,128)(2,1)S(1)}, u32[]{:S(2)}, u32[]{:S(2)}) collective-permute-start(bf16[32,64]{1,0:T(8,128)(2,1)S(1)} %get-tuple-element.42), channel_id=1, source_target_pairs={{1,0},{2,1},{3,2},{4,3},{5,4},{6,5},{7,6},{8,7},{9,8},{10,9},{11,1... | collective-permute-start | bytes 12296 | tf_op jit(solution)/shard_map/ppermute | solution.py:23
  152.8 14.4 %all-to-all-start.2 = ((f32[32,1,512]{2,1,0:T(1,128)}), f32[32,1,512]{2,1,0:T(1,128)S(1)}, u32[]{:S(2)}, u32[]{:S(2)}) async-start(f32[32,1,512]{2,1,0:T(1,128)} %mul.397), calls=%async_computation.2 | async-start | bytes 131072 | tf_op jit(solution)/shard_map/all_to_all | solution.py:42
  205.9 28.5 %all-to-all-start.5 = ((bf16[32,32,512]{2,1,0:T(8,128)(2,1)}), bf16[32,32,512]{2,1,0:T(8,128)(2,1)S(1)}, u32[]{:S(2)}, u32[]{:S(2)}) async-start(bf16[32,32,512]{2,1,0:T(8,128)(2,1)} %broadcast_in_dim.44), calls=%async_computation.5 | async-start | bytes 2097152 | tf_op jit(solution)/shard_map/all_to_all | solution.py:42
  209.9 6.0 %collective-permute-start.2 = (bf16[32,64]{1,0:T(8,128)(2,1)S(1)}, bf16[32,64]{1,0:T(8,128)(2,1)S(1)}, u32[]{:S(2)}, u32[]{:S(2)}) collective-permute-start(bf16[32,64]{1,0:T(8,128)(2,1)S(1)} %get-tuple-element.35), channel_id=1, source_target_pairs={{0,1},{1,2},{2,3},{3,4},{4,5},{5,6},{6,7},{7,8},{8,9},{9,10},{10,1... | collective-permute-start | bytes 12296 | tf_op jit(solution)/shard_map/ppermute | solution.py:21
  213.9 5.3 %collective-permute-start.3 = (bf16[32,64]{1,0:T(8,128)(2,1)S(1)}, bf16[32,64]{1,0:T(8,128)(2,1)S(1)}, u32[]{:S(2)}, u32[]{:S(2)}) collective-permute-start(bf16[32,64]{1,0:T(8,128)(2,1)S(1)} %get-tuple-element.36), channel_id=1, source_target_pairs={{1,0},{2,1},{3,2},{4,3},{5,4},{6,5},{7,6},{8,7},{9,8},{10,9},{11,1... | collective-permute-start | bytes 12296 | tf_op jit(solution)/shard_map/ppermute | solution.py:23
  270.9 28.5 %all-to-all-start.8 = ((bf16[32,32,512]{2,1,0:T(8,128)(2,1)}), bf16[32,32,512]{2,1,0:T(8,128)(2,1)S(1)}, u32[]{:S(2)}, u32[]{:S(2)}) async-start(bf16[32,32,512]{2,1,0:T(8,128)(2,1)} %broadcast_in_dim.47), calls=%async_computation.8 | async-start | bytes 2097152 | tf_op jit(solution)/shard_map/all_to_all | solution.py:42
  274.9 6.0 %collective-permute-start.4 = (bf16[32,64]{1,0:T(8,128)(2,1)S(1)}, bf16[32,64]{1,0:T(8,128)(2,1)S(1)}, u32[]{:S(2)}, u32[]{:S(2)}) collective-permute-start(bf16[32,64]{1,0:T(8,128)(2,1)S(1)} %get-tuple-element.29), channel_id=1, source_target_pairs={{0,1},{1,2},{2,3},{3,4},{4,5},{5,6},{6,7},{7,8},{8,9},{9,10},{10,1... | collective-permute-start | bytes 12296 | tf_op jit(solution)/shard_map/ppermute | solution.py:21
  278.8 5.3 %collective-permute-start.5 = (bf16[32,64]{1,0:T(8,128)(2,1)S(1)}, bf16[32,64]{1,0:T(8,128)(2,1)S(1)}, u32[]{:S(2)}, u32[]{:S(2)}) collective-permute-start(bf16[32,64]{1,0:T(8,128)(2,1)S(1)} %get-tuple-element.30), channel_id=1, source_target_pairs={{1,0},{2,1},{3,2},{4,3},{5,4},{6,5},{7,6},{8,7},{9,8},{10,9},{11,1... | collective-permute-start | bytes 12296 | tf_op jit(solution)/shard_map/ppermute | solution.py:23
Sparse Core Ops, SparseCore 0:
  10.5 117.5 all-gather.1
where the time goes:
time: 343 us; the launch traced here: 342 us
  waiting for transfers between devices  126 us (37%)
  blocking collectives  86.7 us (25%)
  starting transfers between devices  46.1 us (13%)
  local copies, waits for them, and re-layouts  40.7 us (12%)
  matrix products  18.3 us (5%)
  between operations  13.9 us (4%)
  other arithmetic  9.58 us (3%)
    all_to_all x6, blocking collectives, total_over_devices(): rows = lax.all_to_all(spread, axis, split_axis=0, concat_axis=0, tiled=True)  86.7 us
    all_gather x1, waiting for transfers between devices, on_device(): gathered = lax.all_gather(embeddings, 'band', axis=0, tiled=True)  58.1 us
    all_to_all x4, waiting for transfers between devices, band_gather(): lax.all_to_all(spread, 'band', split_axis=0, concat_axis=0, tiled=True)  53.8 us
    all_to_all x4, starting transfers between devices, band_gather(): lax.all_to_all(spread, 'band', split_axis=0, concat_axis=0, tiled=True)  17.5 us
    ppermute x3, starting transfers between devices, with_halo(): lax.ppermute(tail, axis, [(i, (i + 1) % count) for i in range(ends)])  12.1 us
    all_to_all x1, starting transfers between devices, on_device(): lax.all_to_all(ordered, 'band', split_axis=1, concat_axis=1, tiled=True)  10.5 us
    gather x1, local copies, waits for them, and re-layouts, on_device(): partner_rows = gathered.reshape(-1, 128, embed_width)[partners]  9.99 us
    dot_general x3, matrix products, on_device(): jnp.einsum('ctkj,tkji->cti', far_tiles, affinity, preferred_element_type=...  8.82 us
  transfers between devices with their start and end apart: 12, of which 8 were waited for; matrix products, arithmetic and copies ran while one was open for 8% of the time, Pallas kernels for 0%

commit v1 on v0

--- a/solution.py
+++ b/solution.py
@@ -51,7 +51,9 @@
     ordered = jnp.take(seeded, frame_perm[0], axis=1).reshape(
         channels, band_count, frames // band_count
     )
-    arrived = lax.all_to_all(ordered, "band", split_axis=1, concat_axis=1, tiled=True)
+    arrived = jnp.concatenate(
+        lax.all_to_all(jnp.stack(jnp.split(ordered, lax.axis_size("band"), 1)), "band", 0, 0), 1
+    )
     labels = arrived.reshape(channels, frames).astype(jnp.float32)
     device = lax.axis_index("band") * groups + lax.axis_index("seq")
     frame_total = frames * band_count * groups

time: 343 us -> 343 us (level)
  blocking collectives: 86.7 us -> 106 us
  starting transfers between devices: 46.1 us -> 35.6 us
  waiting for transfers between devices: 126 us -> 118 us
    all_to_all x0 -> x1, blocking collectives: none -> 19.1 us  [on_device(): lax.all_to_all(jnp.stack(jnp.split(ordered, lax.axis_size('band'), 1)), '...]
    all_to_all x1 -> x0, starting transfers between devices: 10.5 us -> none  [on_device(): lax.all_to_all(ordered, 'band', split_axis=1, concat_axis=1, tiled=True)]
    all_to_all x1 -> x0, waiting for transfers between devices: 7.39 us -> none  [on_device(): lax.all_to_all(ordered, 'band', split_axis=1, concat_axis=1, tiled=True)]
  transfers between devices with their start and end apart: 12 -> 11, of which waited for: 8 -> 7; matrix products, arithmetic and copies ran while one was open for 8% -> 8% of each run, Pallas kernels for 0% -> 0%
where the time goes in v1:
time: 343 us; the launch traced here: 342 us
  waiting for transfers between devices  118 us (34%)
  blocking collectives  106 us (31%)
  local copies, waits for them, and re-layouts  40.4 us (12%)
  starting transfers between devices  35.6 us (10%)
  matrix products  18.3 us (5%)
  between operations  14 us (4%)
  other arithmetic  10.2 us (3%)
    all_to_all x6, blocking collectives, total_over_devices(): rows = lax.all_to_all(spread, axis, split_axis=0, concat_axis=0, tiled=True)  86.7 us
    all_gather x1, waiting for transfers between devices, on_device(): gathered = lax.all_gather(embeddings, 'band', axis=0, tiled=True)  58.4 us
    all_to_all x4, waiting for transfers between devices, band_gather(): lax.all_to_all(spread, 'band', split_axis=0, concat_axis=0, tiled=True)  52 us
    all_to_all x1, blocking collectives, on_device(): lax.all_to_all(jnp.stack(jnp.split(ordered, lax.axis_size('band'), 1)), '...  19.1 us
    all_to_all x4, starting transfers between devices, band_gather(): lax.all_to_all(spread, 'band', split_axis=0, concat_axis=0, tiled=True)  17.5 us
    ppermute x3, starting transfers between devices, with_halo(): lax.ppermute(tail, axis, [(i, (i + 1) % count) for i in range(ends)])  12.1 us
    gather x1, local copies, waits for them, and re-layouts, on_device(): partner_rows = gathered.reshape(-1, 128, embed_width)[partners]  9.99 us
    dot_general x3, matrix products, on_device(): jnp.einsum('ctkj,tkji->cti', far_tiles, affinity, preferred_element_type=...  8.82 us
  transfers between devices with their start and end apart: 11, of which 7 were waited for; matrix products, arithmetic and copies ran while one was open for 8% of the time, Pallas kernels for 0%

profile of v1, /device:TPU:1, one launch (start us, length us, event | category | flops | bytes accessed | tf_op | source)
XLA Modules:
  0.0 341.7 jit_solution(13605956879348965816)
XLA Ops:
  6.5 0.7 all-gather.2.cloned.1.call-update
  7.3 0.7 convert_element_type.66
  8.0 0.8 broadcast_multiply_fusion
  9.4 1.3 reduce.14
  10.9 0.7 compare_select_fusion.1
  11.6 1.3 gather_fusion
  13.6 19.1 %all_to_all.56 = bf16[32,2,256]{2,1,0:T(2,128)(2,1)S(1)} all-to-all(bf16[32,2,256]{2,1,0:T(2,128)(2,1)S(1)} %reshape.908), channel_id=1, replica_groups=mesh['band'=32,'seq'=16] {'band'}, dimensions={0} | all-to-all | bytes 65536 | tf_op jit(solution)/shard_map/all_to_all | solution.py:55
  32.9 1.2 broadcast_in_dim.40
  34.1 3.9 %all-to-all-start.1 = ((bf16[32,32,512]{2,1,0:T(8,128)(2,1)}), bf16[32,32,512]{2,1,0:T(8,128)(2,1)S(1)}, u32[]{:S(2)}, u32[]{:S(2)}) async-start(bf16[32,32,512]{2,1,0:T(8,128)(2,1)} %broadcast_in_dim.40), calls=%async_computation.1 | async-start | bytes 2097152 | tf_op jit(solution)/shard_map/all_to_all | solution.py:42
  38.0 0.7 compare_select_fusion.3
  38.8 1.0 reduce-window.9
  40.3 4.5 %gather_fusion.1 = s32[1024]{0:T(1024)S(1)} fusion(s32[640]{0:T(1024)S(1)} %convert_reduce_fusion.1, s32[1024]{0:T(1024)S(1)} %get-tuple-element.48), kind=kCustom, calls=%fused_computation.1 | custom fusion | bytes 12288 | tf_op jit(solution)/shard_map/gather | solution.py:72
  45.0 2.3 gather_fusion.2
  47.3 6.8 %gather_fusion.3 = pred[1024]{0:T(1024)(128)(4,1)S(1)} fusion(pred[640]{0:T(1024)(128)(4,1)S(1)} %compare_and_fusion.1, s32[1024]{0:T(1024)S(1)} %get-tuple-element.48), kind=kCustom, calls=%fused_computation.3 | custom fusion | bytes 6144 | tf_op jit(solution)/shard_map/gather | solution.py:73
  54.8 14.9 %all-to-all-done.1 = bf16[32,32,512]{2,1,0:T(8,128)(2,1)S(1)} async-done(((bf16[32,32,512]{2,1,0:T(8,128)(2,1)}), bf16[32,32,512]{2,1,0:T(8,128)(2,1)S(1)}, u32[]{:S(2)}, u32[]{:S(2)}) %all-to-all-start.1) | async-done | bytes 1048608 | tf_op jit(solution)/shard_map/all_to_all | solution.py:42
  69.8 58.4 %all-gather.2.cloned.1.call-done = bf16[16384,256]{1,0:T(8,128)(2,1)} async-done(((bf16[512,256]{1,0:T(8,128)(2,1)}), bf16[16384,256]{1,0:T(8,128)(2,1)}) %all-gather.2.cloned.1.call-update) | async-done | bytes 8388624 | tf_op jit(solution)/shard_map/all_gather | solution.py:79
  128.1 10.0 %gather_fusion.4 = bf16[128,128,256]{2,1,0:T(8,128)(2,1)} fusion(bf16[128,128,256]{2,1,0:T(8,128)(2,1)} %bitcast.343, s32[1024]{0:T(1024)S(1)} %get-tuple-element.45), kind=kCustom, calls=%fused_computation.4 | custom fusion | bytes 16777728 | tf_op jit(solution)/shard_map/gather | solution.py:83
  138.1 7.7 %convert_reduce_fusion = (f32[4,128]{1,0:T(4,128)S(1)}, bf16[4,32,128,128]{3,2,1,0:T(8,128)(2,1)}) fusion(f32[4,32]{1,0:T(4,128)S(1)} %convert_multiply_fusion.6, bf16[4,32,128,256]{3,2,1,0:T(8,128)(2,1)} %bitcast.344, bf16[4,128,256,1]{2,1,3,0:T(8,128)(2,1)S(1)} %bitcast.360), kind=kOutput, calls=%fused_computation.8 | convolution fusion | flops 1086324224 | bytes 12847616 | tf_op jit(solution)/shard_map/tkje,tie->tkji/dot_general | solution.py:85
  145.9 4.2 %collective-permute-start = (bf16[32,64]{1,0:T(8,128)(2,1)S(1)}, bf16[32,64]{1,0:T(8,128)(2,1)S(1)}, u32[]{:S(2)}, u32[]{:S(2)}) collective-permute-start(bf16[32,64]{1,0:T(8,128)(2,1)S(1)} %get-tuple-element.41), channel_id=1, source_target_pairs={{0,1},{1,2},{2,3},{3,4},{4,5},{5,6},{6,7},{7,8},{8,9},{9,10},{10,1... | collective-permute-start | bytes 12296 | tf_op jit(solution)/shard_map/ppermute | solution.py:21
  150.2 1.9 collective-permute-start.1
  152.8 5.7 %all-to-all-start.2 = ((f32[32,1,512]{2,1,0:T(1,128)}), f32[32,1,512]{2,1,0:T(1,128)S(1)}, u32[]{:S(2)}, u32[]{:S(2)}) async-start(f32[32,1,512]{2,1,0:T(1,128)} %mul.415), calls=%async_computation.2 | async-start | bytes 131072 | tf_op jit(solution)/shard_map/all_to_all | solution.py:42
  159.2 7.9 %all-to-all-done.2 = f32[32,1,512]{2,1,0:T(1,128)S(1)} async-done(((f32[32,1,512]{2,1,0:T(1,128)}), f32[32,1,512]{2,1,0:T(1,128)S(1)}, u32[]{:S(2)}, u32[]{:S(2)}) %all-to-all-start.2) | async-done | bytes 65568 | tf_op jit(solution)/shard_map/all_to_all | solution.py:42
  169.3 0.8 gather_fusion.5
  170.1 2.9 fusion.3
  173.5 17.3 %all_to_all.57 = f32[16,1,128]{2,1,0:T(1,128)S(1)} all-to-all(f32[16,1,128]{2,1,0:T(1,128)S(1)} %reshape.910), channel_id=1, replica_groups=mesh['band'=32,'seq'=16] {'seq'}, dimensions={0} | all-to-all | bytes 16384 | tf_op jit(solution)/shard_map/all_to_all | solution.py:34
  192.2 11.6 %all_to_all.58 = f32[32,1,128]{2,1,0:T(1,128)S(1)} all-to-all(f32[32,1,128]{2,1,0:T(1,128)S(1)} %reshape.912), channel_id=1, replica_groups=mesh['band'=32,'seq'=16] {'band'}, dimensions={0} | all-to-all | bytes 32768 | tf_op jit(solution)/shard_map/all_to_all | solution.py:34
  203.8 0.7 reduce.16
  204.8 1.1 broadcast_in_dim.44
  205.9 3.9 %all-to-all-start.5 = ((bf16[32,32,512]{2,1,0:T(8,128)(2,1)}), bf16[32,32,512]{2,1,0:T(8,128)(2,1)S(1)}, u32[]{:S(2)}, u32[]{:S(2)}) async-start(bf16[32,32,512]{2,1,0:T(8,128)(2,1)} %broadcast_in_dim.44), calls=%async_computation.5 | async-start | bytes 2097152 | tf_op jit(solution)/shard_map/all_to_all | solution.py:42
  209.9 4.0 %collective-permute-start.2 = (bf16[32,64]{1,0:T(8,128)(2,1)S(1)}, bf16[32,64]{1,0:T(8,128)(2,1)S(1)}, u32[]{:S(2)}, u32[]{:S(2)}) collective-permute-start(bf16[32,64]{1,0:T(8,128)(2,1)S(1)} %get-tuple-element.35), channel_id=1, source_target_pairs={{0,1},{1,2},{2,3},{3,4},{4,5},{5,6},{6,7},{7,8},{8,9},{9,10},{10,1... | collective-permute-start | bytes 12296 | tf_op jit(solution)/shard_map/ppermute | solution.py:21
  213.9 1.9 collective-permute-start.3
  215.8 3.3 collective-permute-done.3
  219.9 14.5 %all-to-all-done.5 = bf16[32,32,512]{2,1,0:T(8,128)(2,1)S(1)} async-done(((bf16[32,32,512]{2,1,0:T(8,128)(2,1)}), bf16[32,32,512]{2,1,0:T(8,128)(2,1)S(1)}, u32[]{:S(2)}, u32[]{:S(2)}) %all-to-all-start.5) | async-done | bytes 1048608 | tf_op jit(solution)/shard_map/all_to_all | solution.py:42
  236.3 0.8 gather_fusion.6
  237.1 2.9 fusion.2
  240.5 15.1 %all_to_all.59 = f32[16,3,32]{2,1,0:T(4,128)S(1)} all-to-all(f32[16,3,32]{2,1,0:T(4,128)S(1)} %broadcast_in_dim.45), channel_id=1, replica_groups=mesh['band'=32,'seq'=16] {'seq'}, dimensions={0} | all-to-all | bytes 12288 | tf_op jit(solution)/shard_map/all_to_all | solution.py:34
  255.6 14.1 %all_to_all.60 = f32[32,3,32]{2,1,0:T(4,128)S(1)} all-to-all(f32[32,3,32]{2,1,0:T(4,128)S(1)} %broadcast_in_dim.46), channel_id=1, replica_groups=mesh['band'=32,'seq'=16] {'band'}, dimensions={0} | all-to-all | bytes 24576 | tf_op jit(solution)/shard_map/all_to_all | solution.py:34
  269.8 1.1 broadcast_in_dim.47
  270.9 3.9 %all-to-all-start.8 = ((bf16[32,32,512]{2,1,0:T(8,128)(2,1)}), bf16[32,32,512]{2,1,0:T(8,128)(2,1)S(1)}, u32[]{:S(2)}, u32[]{:S(2)}) async-start(bf16[32,32,512]{2,1,0:T(8,128)(2,1)} %broadcast_in_dim.47), calls=%async_computation.8 | async-start | bytes 2097152 | tf_op jit(solution)/shard_map/all_to_all | solution.py:42
  274.9 3.9 %collective-permute-start.4 = (bf16[32,64]{1,0:T(8,128)(2,1)S(1)}, bf16[32,64]{1,0:T(8,128)(2,1)S(1)}, u32[]{:S(2)}, u32[]{:S(2)}) collective-permute-start(bf16[32,64]{1,0:T(8,128)(2,1)S(1)} %get-tuple-element.29), channel_id=1, source_target_pairs={{0,1},{1,2},{2,3},{3,4},{4,5},{5,6},{6,7},{7,8},{8,9},{9,10},{10,1... | collective-permute-start | bytes 12296 | tf_op jit(solution)/shard_map/ppermute | solution.py:21
  278.8 2.1 collective-permute-start.5
  281.0 3.1 collective-permute-done.5
  284.8 14.7 %all-to-all-done.8 = bf16[32,32,512]{2,1,0:T(8,128)(2,1)S(1)} async-done(((bf16[32,32,512]{2,1,0:T(8,128)(2,1)}), bf16[32,32,512]{2,1,0:T(8,128)(2,1)S(1)}, u32[]{:S(2)}, u32[]{:S(2)}) %all-to-all-start.8) | async-done | bytes 1048608 | tf_op jit(solution)/shard_map/all_to_all | solution.py:42
  301.4 0.8 gather_fusion.7
  302.2 2.9 fusion.1
  305.5 14.7 %all_to_all.61 = f32[16,1,32]{2,1,0:T(1,128)S(1)} all-to-all(f32[16,1,32]{2,1,0:T(1,128)S(1)} %broadcast_in_dim.48), channel_id=1, replica_groups=mesh['band'=32,'seq'=16] {'seq'}, dimensions={0} | all-to-all | bytes 4096 | tf_op jit(solution)/shard_map/all_to_all | solution.py:34
  320.2 13.9 %all_to_all.62 = f32[32,1,32]{2,1,0:T(1,128)S(1)} all-to-all(f32[32,1,32]{2,1,0:T(1,128)S(1)} %broadcast_in_dim.49), channel_id=1, replica_groups=mesh['band'=32,'seq'=16] {'band'}, dimensions={0} | all-to-all | bytes 8192 | tf_op jit(solution)/shard_map/all_to_all | solution.py:34
  334.1 0.7 fusion.19
  (126 shorter events, 15.2 us)
Async XLA Ops:
  6.5 48.3 %copy-start.1 = (s32[4,32]{1,0:T(4,128)S(1)}, s32[4,32]{1,0:T(4,128)}, u32[]{:S(2)}) copy-start(s32[4,32]{1,0:T(4,128)} %param.13) | copy-start | bytes 1540
  6.5 121.6 %all-gather.2.cloned.1.call-start = ((), (), s32[]{:S(2)}) async-start(), calls=%async_computation.11 | async-start | bytes 8650752 | tf_op jit(solution)/shard_map/all_gather | solution.py:79
  34.1 35.7 %all-to-all-start.1 = ((bf16[32,32,512]{2,1,0:T(8,128)(2,1)}), bf16[32,32,512]{2,1,0:T(8,128)(2,1)S(1)}, u32[]{:S(2)}, u32[]{:S(2)}) async-start(bf16[32,32,512]{2,1,0:T(8,128)(2,1)} %broadcast_in_dim.40), calls=%async_computation.1 | async-start | bytes 2097152 | tf_op jit(solution)/shard_map/all_to_all | solution.py:42
  128.1 10.0 %copy-start = (bf16[512,256]{1,0:T(8,128)(2,1)S(1)}, bf16[512,256]{1,0:T(8,128)(2,1)}, u32[]{:S(2)}) copy-start(bf16[512,256]{1,0:T(8,128)(2,1)} %param.11) | copy-start | bytes 786436
  145.9 12.6 %collective-permute-start = (bf16[32,64]{1,0:T(8,128)(2,1)S(1)}, bf16[32,64]{1,0:T(8,128)(2,1)S(1)}, u32[]{:S(2)}, u32[]{:S(2)}) collective-permute-start(bf16[32,64]{1,0:T(8,128)(2,1)S(1)} %get-tuple-element.41), channel_id=1, source_target_pairs={{0,1},{1,2},{2,3},{3,4},{4,5},{5,6},{6,7},{7,8},{8,9},{9,10},{10,1... | collective-permute-start | bytes 12296 | tf_op jit(solution)/shard_map/ppermute | solution.py:21
  150.2 8.4 %collective-permute-start.1 = (bf16[32,64]{1,0:T(8,128)(2,1)S(1)}, bf16[32,64]{1,0:T(8,128)(2,1)S(1)}, u32[]{:S(2)}, u32[]{:S(2)}) collective-permute-start(bf16[32,64]{1,0:T(8,128)(2,1)S(1)} %get-tuple-element.42), channel_id=1, source_target_pairs={{1,0},{2,1},{3,2},{4,3},{5,4},{6,5},{7,6},{8,7},{9,8},{10,9},{11,1... | collective-permute-start | bytes 12296 | tf_op jit(solution)/shard_map/ppermute | solution.py:23
  152.8 14.4 %all-to-all-start.2 = ((f32[32,1,512]{2,1,0:T(1,128)}), f32[32,1,512]{2,1,0:T(1,128)S(1)}, u32[]{:S(2)}, u32[]{:S(2)}) async-start(f32[32,1,512]{2,1,0:T(1,128)} %mul.415), calls=%async_computation.2 | async-start | bytes 131072 | tf_op jit(solution)/shard_map/all_to_all | solution.py:42
  205.9 28.5 %all-to-all-start.5 = ((bf16[32,32,512]{2,1,0:T(8,128)(2,1)}), bf16[32,32,512]{2,1,0:T(8,128)(2,1)S(1)}, u32[]{:S(2)}, u32[]{:S(2)}) async-start(bf16[32,32,512]{2,1,0:T(8,128)(2,1)} %broadcast_in_dim.44), calls=%async_computation.5 | async-start | bytes 2097152 | tf_op jit(solution)/shard_map/all_to_all | solution.py:42
  209.9 6.0 %collective-permute-start.2 = (bf16[32,64]{1,0:T(8,128)(2,1)S(1)}, bf16[32,64]{1,0:T(8,128)(2,1)S(1)}, u32[]{:S(2)}, u32[]{:S(2)}) collective-permute-start(bf16[32,64]{1,0:T(8,128)(2,1)S(1)} %get-tuple-element.35), channel_id=1, source_target_pairs={{0,1},{1,2},{2,3},{3,4},{4,5},{5,6},{6,7},{7,8},{8,9},{9,10},{10,1... | collective-permute-start | bytes 12296 | tf_op jit(solution)/shard_map/ppermute | solution.py:21
  213.9 5.3 %collective-permute-start.3 = (bf16[32,64]{1,0:T(8,128)(2,1)S(1)}, bf16[32,64]{1,0:T(8,128)(2,1)S(1)}, u32[]{:S(2)}, u32[]{:S(2)}) collective-permute-start(bf16[32,64]{1,0:T(8,128)(2,1)S(1)} %get-tuple-element.36), channel_id=1, source_target_pairs={{1,0},{2,1},{3,2},{4,3},{5,4},{6,5},{7,6},{8,7},{9,8},{10,9},{11,1... | collective-permute-start | bytes 12296 | tf_op jit(solution)/shard_map/ppermute | solution.py:23
  270.9 28.5 %all-to-all-start.8 = ((bf16[32,32,512]{2,1,0:T(8,128)(2,1)}), bf16[32,32,512]{2,1,0:T(8,128)(2,1)S(1)}, u32[]{:S(2)}, u32[]{:S(2)}) async-start(bf16[32,32,512]{2,1,0:T(8,128)(2,1)} %broadcast_in_dim.47), calls=%async_computation.8 | async-start | bytes 2097152 | tf_op jit(solution)/shard_map/all_to_all | solution.py:42
  274.9 6.0 %collective-permute-start.4 = (bf16[32,64]{1,0:T(8,128)(2,1)S(1)}, bf16[32,64]{1,0:T(8,128)(2,1)S(1)}, u32[]{:S(2)}, u32[]{:S(2)}) collective-permute-start(bf16[32,64]{1,0:T(8,128)(2,1)S(1)} %get-tuple-element.29), channel_id=1, source_target_pairs={{0,1},{1,2},{2,3},{3,4},{4,5},{5,6},{6,7},{7,8},{8,9},{9,10},{10,1... | collective-permute-start | bytes 12296 | tf_op jit(solution)/shard_map/ppermute | solution.py:21
  278.8 5.3 %collective-permute-start.5 = (bf16[32,64]{1,0:T(8,128)(2,1)S(1)}, bf16[32,64]{1,0:T(8,128)(2,1)S(1)}, u32[]{:S(2)}, u32[]{:S(2)}) collective-permute-start(bf16[32,64]{1,0:T(8,128)(2,1)S(1)} %get-tuple-element.30), channel_id=1, source_target_pairs={{1,0},{2,1},{3,2},{4,3},{5,4},{6,5},{7,6},{8,7},{9,8},{10,9},{11,1... | collective-permute-start | bytes 12296 | tf_op jit(solution)/shard_map/ppermute | solution.py:23
Sparse Core Ops, SparseCore 0:
  10.5 117.5 all-gather.1
